TPU v7x, 32 devices: a whole 2x2x4 slice. The times are simulated.
32 devices in a mesh: groups: 2 (over y), rows: 8 (over z, x), heads: 2 (over core).
Axes of the slice: x: 2, y: 2, z: 4, core: 2. Of those that a mesh axis runs over, the one named last changes fastest.
Arguments:
- residual_in: bfloat16 [128, 8192], P(('groups', 'rows'), 'heads'), parts along dimension 0, may hold values from -6 to 6
- query: bfloat16 [128, 8192], P(('groups', 'rows'), 'heads'), parts along dimension 0, may hold values from -120 to 120
- key_cache: bfloat16 [128, 4, 32, 128], P(('groups', 'rows'), 'heads'), parts along dimension 0, may hold values from -4 to 4
- value_cache: bfloat16 [128, 4, 32, 128], P(('groups', 'rows'), 'heads'), parts along dimension 0, may hold values from -5 to 5
- key_new: bfloat16 [128, 4, 128], P(('groups', 'rows'), 'heads'), parts along dimension 0, may hold values from -4 to 4
- value_new: bfloat16 [128, 4, 128], P(('groups', 'rows'), 'heads'), parts along dimension 0, may hold values from -5 to 5
- lengths: int32 [128], P(('groups', 'rows')), parts along dimension 0, may hold values from 2 to 32, as said below
- norm_gain: bfloat16 [8192], replicated, may hold values from 0.3984375 to 1.59375
- hot_gate: bfloat16 [128, 8192], P('heads'), may hold values from -0.0625 to 0.0625
- hot_up: bfloat16 [128, 8192], P('heads'), may hold values from -0.0625 to 0.0625
- hot_down: bfloat16 [128, 8192], P('heads'), may hold values from -0.5 to 0.5
- cold_gate: bfloat16 [512, 8192], P(('rows', 'heads')), may hold values from -0.0625 to 0.0625
- cold_up: bfloat16 [512, 8192], P(('rows', 'heads')), may hold values from -0.0625 to 0.0625
- cold_down: bfloat16 [512, 8192], P(('rows', 'heads')), may hold values from -0.5 to 0.5
- active: int32 [128, 4], P(('groups', 'rows')), parts along dimension 0, may hold values from 0 to 1, as said below
Outputs:
- residual_out: bfloat16 [128, 8192], P(('groups', 'rows'), 'heads'), parts along dimension 0
There are 2 independent parts, one for each index of `groups`. A program takes and returns all parts, laid end to end along the dimension named above; an argument that names none is the same for every part. Nothing has to cross between parts.
Inputs may be any that keep to these rules, and one draw needn't show every extreme that they name: `lengths`: every request has at least two filled slots, and some request has all 32. `active`: 0 or 1; among the 8 requests of one index of rows at most 2 are active on any one cold block, and exactly 2 on some.
All inputs are finite; a program needn't handle non-finite values.
Results may differ from a plain program's by a relative error of at most 0.0085.
Values may be sent and summed in bfloat16 or wider, within the bound.
No kernel may reach another device: no remote copies, remote signals or barrier semaphores. Data moves between devices by JAX's collectives and lax.ppermute only.
A program may use at most 64 MiB of HBM per device.

v0:
```python
import jax
import jax.numpy as jnp
from jax import lax
from jax.sharding import PartitionSpec as P

HD = 128
D = 8192
CAP = 2


def partner(block, axis, bit):
    count = lax.axis_size(axis)
    route = []
    for low in range(count):
        high = low | 1 << bit
        if high != low and high < count:
            route += [(low, high), (high, low)]
    return lax.ppermute(block, axis, route)


def join_halves(half, myself):
    other = partner(half, "heads", 0)
    low_first = jnp.concatenate([half, other], axis=1)
    high_first = jnp.concatenate([other, half], axis=1)
    return jnp.where(myself == 0, low_first, high_first)


def attention_rows(query, key_cache, value_cache, key_new, value_new, lengths):
    count = key_cache.shape[0]
    kv_local = key_cache.shape[1]
    scale_factor = 1.0 / HD**0.5
    queries = query.reshape(count, kv_local, -1, HD)
    scores = (
        jnp.einsum("rgjd,rgpd->rgjp", queries, key_cache, preferred_element_type=jnp.float32)
        * scale_factor
    )
    own_score = (
        jnp.einsum("rgjd,rgd->rgj", queries, key_new, preferred_element_type=jnp.float32)
        * scale_factor
    )
    visible = (jnp.arange(key_cache.shape[2], dtype=jnp.int32)[None, :] < lengths[:, None])[
        :, None, None, :
    ]
    scores = jnp.where(visible, scores, -1e30)
    highest = jnp.maximum(jnp.max(scores, axis=-1), own_score)
    expons = jnp.where(visible, jnp.exp(scores - highest[..., None]), 0.0)
    own_expon = jnp.exp(own_score - highest)
    totals = jnp.sum(expons, axis=-1) + own_expon
    weights = (expons / totals[..., None]).astype(jnp.bfloat16)
    own_weight = (own_expon / totals).astype(jnp.bfloat16)
    blended = jnp.einsum(
        "rgjp,rgpd->rgjd", weights, value_cache, preferred_element_type=jnp.float32
    )
    blended = (
        blended
        + own_weight.astype(jnp.float32)[..., None] * value_new.astype(jnp.float32)[:, :, None, :]
    )
    return blended.reshape(count, -1)


def swiglu_rows(normed, gate_rows, up_rows, down_rows):
    gate = jnp.einsum("rd,nd->rn", normed, gate_rows, preferred_element_type=jnp.float32)
    upper = jnp.einsum("rd,nd->rn", normed, up_rows, preferred_element_type=jnp.float32)
    hidden = (jax.nn.silu(gate) * upper).astype(jnp.bfloat16)
    return jnp.dot(hidden, down_rows, preferred_element_type=jnp.float32)


def collect_rows(selector, returned):
    return lax.dot_general(
        selector,
        returned,
        (((0,), (0,)), ((), ())),
        precision=lax.Precision.HIGHEST,
        preferred_element_type=jnp.float32,
    )


def local(
    residual_in,
    query,
    key_cache,
    value_cache,
    key_new,
    value_new,
    lengths,
    norm_gain,
    hot_gate,
    hot_up,
    hot_down,
    cold_gate,
    cold_up,
    cold_down,
    active,
):
    attended = attention_rows(query, key_cache, value_cache, key_new, value_new, lengths)
    stream = (residual_in.astype(jnp.float32) + attended).astype(jnp.bfloat16)
    half_width = stream.shape[1]
    myself = lax.axis_index("heads")
    local_wide = stream.astype(jnp.float32)
    square_part = jnp.sum(local_wide * local_wide, axis=-1)
    square_total = square_part + partner(square_part, "heads", 0)
    gain_half = lax.dynamic_slice_in_dim(norm_gain, myself * half_width, half_width)
    scaled = (
        local_wide * lax.rsqrt(square_total / D + 1e-05)[:, None] * gain_half.astype(jnp.float32)
    )
    normed = join_halves(scaled.astype(jnp.bfloat16), myself)
    hot_part = swiglu_rows(normed, hot_gate, hot_up, hot_down)
    owner_count = lax.axis_size("rows")
    block_count = active.shape[1]
    request_count = active.shape[0]
    by_block = jnp.transpose(active)
    earlier = jnp.cumsum(by_block, axis=1) - by_block
    slot_ids = jnp.arange(CAP, dtype=jnp.int32)[None, :, None]
    slot_table = by_block[:, None, :] * (earlier[:, None, :] == slot_ids).astype(jnp.int32)
    selector = jnp.repeat(slot_table, owner_count // block_count, axis=0).reshape(
        owner_count * CAP, request_count
    )
    outgoing = jnp.dot(
        selector.astype(jnp.bfloat16), normed, preferred_element_type=jnp.float32
    ).astype(jnp.bfloat16)
    incoming = lax.all_to_all(outgoing, "rows", split_axis=0, concat_axis=0, tiled=True)
    cold_part = swiglu_rows(incoming, cold_gate, cold_up, cold_down)
    selector_wide = selector.astype(jnp.float32)
    kept = lax.dynamic_slice_in_dim(cold_part, myself * half_width, half_width, 1)
    given = lax.dynamic_slice_in_dim(cold_part, (1 - myself) * half_width, half_width, 1)
    owner_sum = kept + partner(given, "heads", 0)
    returned = lax.all_to_all(owner_sum, "rows", split_axis=0, concat_axis=0, tiled=True)
    cold_sum = collect_rows(selector_wide, returned)
    hot_kept = lax.dynamic_slice_in_dim(hot_part, myself * half_width, half_width, 1)
    hot_given = lax.dynamic_slice_in_dim(hot_part, (1 - myself) * half_width, half_width, 1)
    hot_total = hot_kept + partner(hot_given, "heads", 0)
    result = stream.astype(jnp.float32) + hot_total + cold_sum
    return result.astype(jnp.bfloat16)


def solution(mesh):
    return jax.shard_map(
        local,
        mesh=mesh,
        in_specs=(
            P(("groups", "rows"), "heads"),
            P(("groups", "rows"), "heads"),
            P(("groups", "rows"), "heads", None, None),
            P(("groups", "rows"), "heads", None, None),
            P(("groups", "rows"), "heads", None),
            P(("groups", "rows"), "heads", None),
            P(("groups", "rows")),
            P(),
            P("heads", None),
            P("heads", None),
            P("heads", None),
            P(("rows", "heads"), None),
            P(("rows", "heads"), None),
            P(("rows", "heads"), None),
            P(("groups", "rows"), None),
        ),
        out_specs=P(("groups", "rows"), "heads"),
        check_vma=False,
    )
```

profile of v0, /device:TPU:0, one launch (start us, length us, event | category | flops | bytes accessed | tf_op | source)
XLA Modules:
  0.0 45.1 jit_solution(7972570449464875627)
XLA Ops:
  0.0 0.0 copy-start
  0.0 0.0 copy-start.4
  0.0 0.8 %iota_compare_fusion = pred[8,32]{1,0:T(8,128)(4,1)S(1)} fusion(s32[8]{0:T(128)} %param.21), kind=kLoop, calls=%fused_computation.44 | loop fusion | flops 256 | bytes 288 | tf_op jit(solution)/shard_map/lt | solution.py:41
  0.8 1.0 %fusion.14 = f32[8,2,1,16]{3,2,1,0:T(1,128)S(1)} fusion(bf16[8,2,16,128]{3,0,2,1:T(8,128)(2,1)} %bitcast.29, bf16[8,2,128,1]{2,1,0,3:T(2,128)(2,1)} %bitcast.37), kind=kOutput, calls=%fused_computation.26 | convolution fusion | flops 65536 | bytes 70656 | tf_op jit(solution)/shard_map/rgjd,rgd->rgj/dot_general | solution.py:38
  1.8 0.0 copy-done.4
  1.8 1.2 %fusion.36 = (f32[8,2,16]{2,1,0:T(2,128)S(1)}, f32[8,2,16,32]{3,2,1,0:T(8,128)S(1)}) fusion(bf16[8,2,32,128]{3,2,1,0:T(8,128)(2,1)} %param.17, bf16[8,2,16,128]{3,0,2,1:T(8,128)(2,1)S(1)} %bitcast.30, pred[8,32]{1,0:T(8,128)(4,1)S(1)} %iota_compare_fusion), kind=kOutput, calls=%fused_computation.58 | convolution fusion | flops 2121472 | bytes 230656 | tf_op jit(solution)/shard_map/rgjd,rgpd->rgjp/dot_general | solution.py:34
  3.0 0.0 copy-start.9
  3.0 0.2 fusion.9
  3.3 0.0 copy-start.8
  3.3 0.7 %copy-done.8 = bf16[8,2,128]{2,1,0:T(2,128)(2,1)S(1)} copy-done((bf16[8,2,128]{2,1,0:T(2,128)(2,1)S(1)}, bf16[8,2,128]{2,1,0:T(2,128)(2,1)}, u32[]{:S(2)}) %copy-start.8) | copy-done | bytes 4120
  4.0 0.0 copy-done.9
  4.0 0.0 copy-start.5
  4.0 0.0 copy-start.6
  4.0 0.3 convolution_add_fusion
  4.2 0.0 copy-start.7
  4.2 0.5 %copy-done.5 = bf16[8,4096]{1,0:T(8,128)(2,1)S(1)} copy-done((bf16[8,4096]{1,0:T(8,128)(2,1)S(1)}, bf16[8,4096]{1,0:T(8,128)(2,1)}, u32[]{:S(2)}) %copy-start.5) | copy-done | bytes 65560
  4.8 0.2 fusion.3
  5.0 0.5 %collective-permute-start = (f32[8]{0:T(128)S(1)}, f32[8]{0:T(128)S(1)}, u32[]{:S(2)}, u32[]{:S(2)}) collective-permute-start(f32[8]{0:T(128)S(1)} %get-tuple-element.5), channel_id=1, source_target_pairs={{0,1},{1,0},{2,3},{3,2},{4,5},{5,4},{6,7},{7,6},{8,9},{9,8},{10,11... | collective-permute-start | bytes 104 | tf_op jit(solution)/shard_map/ppermute | solution.py:18
  5.5 0.0 copy-done.6
  5.5 0.2 reduce_window_sum.11
  5.7 0.0 copy-done.7
  5.7 0.6 %collective-permute-done = f32[8]{0:T(128)S(1)} collective-permute-done((f32[8]{0:T(128)S(1)}, f32[8]{0:T(128)S(1)}, u32[]{:S(2)}, u32[]{:S(2)}) %collective-permute-start) | collective-permute-done | bytes 64 | tf_op jit(solution)/shard_map/ppermute | solution.py:18
  6.3 0.1 fusion.5
  6.4 0.4 collective-permute-start.1
  6.8 0.9 %collective-permute-done.1 = bf16[8,4096]{1,0:T(8,128)(2,1)S(1)} collective-permute-done((bf16[8,4096]{1,0:T(8,128)(2,1)S(1)}, bf16[8,4096]{1,0:T(8,128)(2,1)S(1)}, u32[]{:S(2)}, u32[]{:S(2)}) %collective-permute-start.1) | collective-permute-done | bytes 65568 | tf_op jit(solution)/shard_map/ppermute | solution.py:18
  7.7 0.2 convolution_convert_fusion
  8.0 0.9 %all_to_all.16 = bf16[8,2,8192]{2,1,0:T(2,128)(2,1)} reshape(bf16[16,8192]{1,0:T(8,128)(2,1)S(1)} %convolution_convert_fusion) | data formatting | bytes 524288 | tf_op jit(solution)/shard_map/all_to_all | solution.py:121
  8.9 7.1 %all-to-all-start = ((bf16[8,2,8192]{2,1,0:T(2,128)(2,1)}), bf16[8,2,8192]{2,1,0:T(2,128)(2,1)S(1)}, u32[]{:S(2)}, u32[]{:S(2)}) async-start(bf16[8,2,8192]{2,1,0:T(2,128)(2,1)} %all_to_all.16), calls=%async_computation | async-start | bytes 524288 | tf_op jit(solution)/shard_map/all_to_all | solution.py:121
  16.0 0.0 copy-done.1
  16.0 0.4 fusion.33
  16.3 8.9 %all-to-all-done = bf16[8,2,8192]{2,1,0:T(2,128)(2,1)S(1)} async-done(((bf16[8,2,8192]{2,1,0:T(2,128)(2,1)}), bf16[8,2,8192]{2,1,0:T(2,128)(2,1)S(1)}, u32[]{:S(2)}, u32[]{:S(2)}) %all-to-all-start) | async-done | bytes 262176 | tf_op jit(solution)/shard_map/all_to_all | solution.py:121
  25.3 0.1 all_to_all.18
  25.4 0.0 copy-done.3
  25.4 0.2 fusion.37
  25.6 1.9 %fusion.2 = f32[16,8192]{1,0:T(8,128)S(1)} fusion(bf16[32,8192]{1,0:T(8,128)(2,1)} %param.28, bf16[16,8192]{1,0:T(8,128)(2,1)S(1)} %all_to_all.18, bf16[32,8192]{1,0:T(8,128)(2,1)} %param.27, f32[16,32]{1,0:T(8,128)S(1)} %fusion.37), kind=kOutput, calls=%fused_computation.6 | convolution fusion | flops 16780288 | bytes 1837056 | tf_op jit(solution)/shard_map/dot_general | solution.py:65
  27.5 0.1 collective-permute-start.3
  27.6 0.0 copy-done
  27.6 0.0 copy-done.2
  27.6 0.9 %fusion.27 = f32[8,8192]{1,0:T(8,128)S(1)} fusion(bf16[64,8192]{1,0:T(8,128)(2,1)S(1)} %copy-done, f32[8,64]{1,0:T(8,128)S(1)} %fusion.33, bf16[64,8192]{1,0:T(8,128)(2,1)S(1)} %copy-done.2, bf16[8,4096]{1,0:T(8,128)(2,1)S(1)} %collective-permute-done.1, bf16[8,4096]{1,0:T(8,128)(2,1)S(1)} %fusion.5, pred[]{:T(512)S(6)} %eq.16), kind=kOutput, calls=%fused_computation.46 | convolution fusion | flops 17370112 | bytes 2492417 | tf_op jit(solution)/shard_map/dot_general | solution.py:65
  28.5 0.7 %collective-permute-done.3 = f32[16,4096]{1,0:T(8,128)} collective-permute-done((f32[16,4096]{1,0:T(8,128)S(1)}, f32[16,4096]{1,0:T(8,128)}, u32[]{:S(2)}, u32[]{:S(2)}) %collective-permute-start.3) | collective-permute-done | bytes 262176 | tf_op jit(solution)/shard_map/ppermute | solution.py:18
  29.3 1.0 %dynamic-slice_add_fusion = f32[16,4096]{1,0:T(8,128)S(1)} fusion(f32[16,4096]{1,0:T(8,128)} %collective-permute-done.3, f32[16,8192]{1,0:T(8,128)S(1)} %fusion.2, s32[]{:T(128)S(6)} %select_n.27), kind=kLoop, calls=%fused_computation.7 | loop fusion | flops 65536 | bytes 786436 | tf_op jit(solution)/shard_map/add | solution.py:126
  30.2 0.9 %all_to_all.19 = f32[8,2,4096]{2,1,0:T(2,128)} reshape(f32[16,4096]{1,0:T(8,128)S(1)} %dynamic-slice_add_fusion) | data formatting | bytes 524288 | tf_op jit(solution)/shard_map/all_to_all | solution.py:127
  31.1 3.6 %all-to-all-start.1 = ((f32[8,2,4096]{2,1,0:T(2,128)}), f32[8,2,4096]{2,1,0:T(2,128)S(1)}, u32[]{:S(2)}, u32[]{:S(2)}) async-start(f32[8,2,4096]{2,1,0:T(2,128)} %all_to_all.19), calls=%async_computation.1 | async-start | bytes 524288 | tf_op jit(solution)/shard_map/all_to_all | solution.py:127
  34.7 0.1 collective-permute-start.2
  34.8 9.2 %all-to-all-done.1 = f32[8,2,4096]{2,1,0:T(2,128)S(1)} async-done(((f32[8,2,4096]{2,1,0:T(2,128)}), f32[8,2,4096]{2,1,0:T(2,128)S(1)}, u32[]{:S(2)}, u32[]{:S(2)}) %all-to-all-start.1) | async-done | bytes 262176 | tf_op jit(solution)/shard_map/all_to_all | solution.py:127
  44.0 0.2 all_to_all.21
  44.1 0.0 collective-permute-done.2
  44.2 1.0 %fusion.7 = bf16[8,4096]{1,0:T(8,128)(2,1)} fusion(bf16[8,4096]{1,0:T(8,128)(2,1)S(1)} %get-tuple-element.6, f32[8,4096]{1,0:T(8,128)S(1)} %collective-permute-done.2, f32[8,8192]{1,0:T(8,128)S(1)} %fusion.27, s32[]{:T(128)S(6)} %select_n.27, f32[16,8]{1,0:T(8,128)S(1)} %bitcast.31, f32[16,4096]{1,0:T(8,128)S(1)} %all_to_all.21), kind=kOutput, calls=%fused_computation.15 | convolution fusion | flops 6455296 | bytes 655876 | tf_op jit(solution)/shard_map/dot_general | solution.py:69
  (14 shorter events, 0.1 us)
Async XLA Ops:
  0.0 27.6 %copy-start = (bf16[64,8192]{1,0:T(8,128)(2,1)S(1)}, bf16[64,8192]{1,0:T(8,128)(2,1)}, u32[]{:S(2)}) copy-start(bf16[64,8192]{1,0:T(8,128)(2,1)} %param.25) | copy-start | bytes 3145732
  0.0 1.8 %copy-start.4 = (bf16[8,4096]{1,0:T(8,128)(2,1)S(1)}, bf16[8,4096]{1,0:T(8,128)(2,1)}, u32[]{:S(2)}) copy-start(bf16[8,4096]{1,0:T(8,128)(2,1)} %param.16) | copy-start | bytes 196612
  3.0 1.0 %copy-start.9 = (bf16[8,2,32,128]{3,2,1,0:T(8,128)(2,1)S(1)}, bf16[8,2,32,128]{3,2,1,0:T(8,128)(2,1)}, u32[]{:S(2)}) copy-start(bf16[8,2,32,128]{3,2,1,0:T(8,128)(2,1)} %param.18) | copy-start | bytes 393220
  3.3 0.7 %copy-start.8 = (bf16[8,2,128]{2,1,0:T(2,128)(2,1)S(1)}, bf16[8,2,128]{2,1,0:T(2,128)(2,1)}, u32[]{:S(2)}) copy-start(bf16[8,2,128]{2,1,0:T(2,128)(2,1)} %param.20) | copy-start | bytes 12292
  4.0 0.8 %copy-start.5 = (bf16[8,4096]{1,0:T(8,128)(2,1)S(1)}, bf16[8,4096]{1,0:T(8,128)(2,1)}, u32[]{:S(2)}) copy-start(bf16[8,4096]{1,0:T(8,128)(2,1)} %param.15) | copy-start | bytes 196612
  4.0 1.5 %copy-start.6 = (s32[8,4]{0,1:T(4,128)S(1)}, s32[8,4]{0,1:T(4,128)}, u32[]{:S(2)}) copy-start(s32[8,4]{0,1:T(4,128)} %param.29) | copy-start | bytes 388
  4.2 1.5 %copy-start.7 = (bf16[8192]{0:T(1024)(128)(2,1)S(1)}, bf16[8192]{0:T(1024)(128)(2,1)}, u32[]{:S(2)}) copy-start(bf16[8192]{0:T(1024)(128)(2,1)} %param.22) | copy-start | bytes 49156
  4.8 11.2 %copy-start.1 = (bf16[64,8192]{1,0:T(8,128)(2,1)S(1)}, bf16[64,8192]{1,0:T(8,128)(2,1)}, u32[]{:S(2)}) copy-start(bf16[64,8192]{1,0:T(8,128)(2,1)} %param.24) | copy-start | bytes 3145732
  5.0 1.3 %collective-permute-start = (f32[8]{0:T(128)S(1)}, f32[8]{0:T(128)S(1)}, u32[]{:S(2)}, u32[]{:S(2)}) collective-permute-start(f32[8]{0:T(128)S(1)} %get-tuple-element.5), channel_id=1, source_target_pairs={{0,1},{1,0},{2,3},{3,2},{4,5},{5,4},{6,7},{7,6},{8,9},{9,8},{10,11... | collective-permute-start | bytes 104 | tf_op jit(solution)/shard_map/ppermute | solution.py:18
  6.4 1.3 %collective-permute-start.1 = (bf16[8,4096]{1,0:T(8,128)(2,1)S(1)}, bf16[8,4096]{1,0:T(8,128)(2,1)S(1)}, u32[]{:S(2)}, u32[]{:S(2)}) collective-permute-start(bf16[8,4096]{1,0:T(8,128)(2,1)S(1)} %fusion.5), channel_id=1, source_target_pairs={{0,1},{1,0},{2,3},{3,2},{4,5},{5,4},{6,7},{7,6},{8,9},{9,8},{10,11... | collective-permute-start | bytes 196616 | tf_op jit(solution)/shard_map/ppermute | solution.py:18
  8.9 16.4 %all-to-all-start = ((bf16[8,2,8192]{2,1,0:T(2,128)(2,1)}), bf16[8,2,8192]{2,1,0:T(2,128)(2,1)S(1)}, u32[]{:S(2)}, u32[]{:S(2)}) async-start(bf16[8,2,8192]{2,1,0:T(2,128)(2,1)} %all_to_all.16), calls=%async_computation | async-start | bytes 524288 | tf_op jit(solution)/shard_map/all_to_all | solution.py:121
  16.3 9.0 %copy-start.3 = (bf16[32,8192]{1,0:T(8,128)(2,1)S(1)}, bf16[32,8192]{1,0:T(8,128)(2,1)}, u32[]{:S(2)}) copy-start(bf16[32,8192]{1,0:T(8,128)(2,1)} %param.26) | copy-start | bytes 1572868
  25.6 2.0 %copy-start.2 = (bf16[64,8192]{1,0:T(8,128)(2,1)S(1)}, bf16[64,8192]{1,0:T(8,128)(2,1)}, u32[]{:S(2)}) copy-start(bf16[64,8192]{1,0:T(8,128)(2,1)} %param.23) | copy-start | bytes 3145732
  27.5 1.7 %collective-permute-start.3 = (f32[16,4096]{1,0:T(8,128)S(1)}, f32[16,4096]{1,0:T(8,128)}, u32[]{:S(2)}, u32[]{:S(2)}) collective-permute-start(f32[16,4096]{1,0:T(8,128)S(1)} %constant_dynamic-slice_fusion), channel_id=1, source_target_pairs={{0,1},{1,0},{2,3},{3,2},{4,5},{5,4},{6,7},{7,6},{8,9},{9,8},{10,11... | collective-permute-start | bytes 786440 | tf_op jit(solution)/shard_map/ppermute | solution.py:18
  31.1 12.9 %all-to-all-start.1 = ((f32[8,2,4096]{2,1,0:T(2,128)}), f32[8,2,4096]{2,1,0:T(2,128)S(1)}, u32[]{:S(2)}, u32[]{:S(2)}) async-start(f32[8,2,4096]{2,1,0:T(2,128)} %all_to_all.19), calls=%async_computation.1 | async-start | bytes 524288 | tf_op jit(solution)/shard_map/all_to_all | solution.py:127
  34.7 9.4 %collective-permute-start.2 = (f32[8,4096]{1,0:T(8,128)S(1)}, f32[8,4096]{1,0:T(8,128)S(1)}, u32[]{:S(2)}, u32[]{:S(2)}) collective-permute-start(f32[8,4096]{1,0:T(8,128)S(1)} %constant_dynamic-slice_fusion.1), channel_id=1, source_target_pairs={{0,1},{1,0},{2,3},{3,2},{4,5},{5,4},{6,7},{7,6},{8,9},{9,8},{10,11... | collective-permute-start | bytes 393224 | tf_op jit(solution)/shard_map/ppermute | solution.py:18
where the time goes:
time: 45.6 us; the launch traced here: 45.1 us
  waiting for transfers between devices  20.4 us (45%)
  starting transfers between devices  11.7 us (26%)
  matrix products  6.98 us (15%)
  local copies, waits for them, and re-layouts  3.33 us (7%)
  other arithmetic  2.53 us (6%)
    all_to_all x1, waiting for transfers between devices, local(): lax.all_to_all(owner_sum, 'rows', split_axis=0, concat_axis=0, tiled=True)  9.17 us
    all_to_all x1, waiting for transfers between devices, local(): lax.all_to_all(outgoing, 'rows', split_axis=0, concat_axis=0, tiled=True)  8.91 us
    all_to_all x1, starting transfers between devices, local(): lax.all_to_all(outgoing, 'rows', split_axis=0, concat_axis=0, tiled=True)  7.1 us
    all_to_all x1, starting transfers between devices, local(): lax.all_to_all(owner_sum, 'rows', split_axis=0, concat_axis=0, tiled=True)  3.59 us
    dot_general x2, matrix products, swiglu_rows(): return jnp.dot(hidden, down_rows, preferred_element_type=jnp.float32)  2.78 us
    ppermute x4, waiting for transfers between devices, partner(): return lax.ppermute(block, axis, route)  2.3 us
    unnamed x20, local copies, waits for them, and re-layouts  1.24 us
    dot_general x1, matrix products, attention_rows(): jnp.einsum('rgjd,rgpd->rgjp', queries, key_cache, preferred_element_type=...  1.17 us
  transfers between devices with their start and end apart: 6, of which 5 were waited for; matrix products, arithmetic and copies ran while one was open for 3% of the time, Pallas kernels for 0%

commit v1 on v0

--- a/solution.py
+++ b/solution.py
@@ -6,6 +6,17 @@
 HD = 128
 D = 8192
 CAP = 2
+
+
+def play_limits(z, dim_k, field_in):
+    m_next, passed = (z.shape[:dim_k], z.shape[dim_k + 1 :])
+    return jnp.moveaxis(z.reshape(*m_next, field_in, -1, *passed), dim_k, 0)
+
+
+def deliver_the_lots_all(arr, along_dim):
+    heard = list(arr.shape[1:])
+    heard[along_dim] *= arr.shape[0]
+    return jnp.moveaxis(arr, 0, along_dim).reshape(heard)
 
 
 def partner(block, axis, bit):
@@ -124,7 +135,14 @@
     kept = lax.dynamic_slice_in_dim(cold_part, myself * half_width, half_width, 1)
     given = lax.dynamic_slice_in_dim(cold_part, (1 - myself) * half_width, half_width, 1)
     owner_sum = kept + partner(given, "heads", 0)
-    returned = lax.all_to_all(owner_sum, "rows", split_axis=0, concat_axis=0, tiled=True)
+    local_next, left_arr = (lax.axis_size("rows"), lax.axis_index("rows"))
+    x_new = play_limits(owner_sum, 0, local_next)
+    line_up = [x_new[left_arr]]
+    for num in range(1, local_next):
+        e_now = x_new[left_arr ^ num]
+        line_up.append(lax.ppermute(e_now, "rows", [(k0, k0 ^ num) for k0 in range(local_next)]))
+    x_new = jnp.stack(line_up)[left_arr ^ jnp.arange(local_next)]
+    returned = deliver_the_lots_all(x_new, 0)
     cold_sum = collect_rows(selector_wide, returned)
     hot_kept = lax.dynamic_slice_in_dim(hot_part, myself * half_width, half_width, 1)
     hot_given = lax.dynamic_slice_in_dim(hot_part, (1 - myself) * half_width, half_width, 1)

time: 45.6 us -> 48.6 us (1.066)
  starting transfers between devices: 11.7 us -> 19.5 us
  waiting for transfers between devices: 20.4 us -> 15.3 us
    ppermute x0 -> x7, starting transfers between devices: none -> 11.4 us  [local(): lax.ppermute(e_now, 'rows', [(k0, k0 ^ num) for k0 in range(local_next)])]
    all_to_all x1 -> x0, waiting for transfers between devices: 9.17 us -> none  [local(): lax.all_to_all(owner_sum, 'rows', split_axis=0, concat_axis=0, tiled=True)]
    ppermute x0 -> x7, waiting for transfers between devices: none -> 4.15 us  [local(): lax.ppermute(e_now, 'rows', [(k0, k0 ^ num) for k0 in range(local_next)])]
    all_to_all x1 -> x0, starting transfers between devices: 3.59 us -> none  [local(): lax.all_to_all(owner_sum, 'rows', split_axis=0, concat_axis=0, tiled=True)]
    all_to_all x2 -> x0, local copies, waits for them, and re-layouts: 1.04 us -> none  [local(): lax.all_to_all(owner_sum, 'rows', split_axis=0, concat_axis=0, tiled=True)]
    gather x0 -> x1, local copies, waits for them, and re-layouts: none -> 0.83 us  [local(): x_new = jnp.stack(line_up)[left_arr ^ jnp.arange(local_next)]]
    unnamed x20 -> x26, local copies, waits for them, and re-layouts: 1.24 us -> 1.3 us
  transfers between devices with their start and end apart: 6 -> 12, of which waited for: 5 -> 6; matrix products, arithmetic and copies ran while one was open for 3% -> 5% of each run, Pallas kernels for 0% -> 0%
where the time goes in v1:
time: 48.6 us; the launch traced here: 48.2 us
  starting transfers between devices  19.5 us (40%)
  waiting for transfers between devices  15.3 us (31%)
  matrix products  6.98 us (14%)
  local copies, waits for them, and re-layouts  3.54 us (7%)
  other arithmetic  2.55 us (5%)
    ppermute x7, starting transfers between devices, local(): lax.ppermute(e_now, 'rows', [(k0, k0 ^ num) for k0 in range(local_next)])  11.4 us
    all_to_all x1, waiting for transfers between devices, local(): lax.all_to_all(outgoing, 'rows', split_axis=0, concat_axis=0, tiled=True)  8.89 us
    all_to_all x1, starting transfers between devices, local(): lax.all_to_all(outgoing, 'rows', split_axis=0, concat_axis=0, tiled=True)  7.1 us
    ppermute x7, waiting for transfers between devices, local(): lax.ppermute(e_now, 'rows', [(k0, k0 ^ num) for k0 in range(local_next)])  4.15 us
    dot_general x2, matrix products, swiglu_rows(): return jnp.dot(hidden, down_rows, preferred_element_type=jnp.float32)  2.78 us
    ppermute x4, waiting for transfers between devices, partner(): return lax.ppermute(block, axis, route)  2.3 us
    unnamed x26, local copies, waits for them, and re-layouts  1.3 us
    dot_general x1, matrix products, attention_rows(): jnp.einsum('rgjd,rgpd->rgjp', queries, key_cache, preferred_element_type=...  1.17 us
  transfers between devices with their start and end apart: 12, of which 6 were waited for; matrix products, arithmetic and copies ran while one was open for 5% of the time, Pallas kernels for 0%

profile of v1, /device:TPU:0, one launch (start us, length us, event | category | flops | bytes accessed | tf_op | source)
XLA Modules:
  0.0 48.2 jit_solution(908897301201448206)
XLA Ops:
  0.0 0.8 %iota_compare_fusion = pred[8,32]{1,0:T(8,128)(4,1)S(1)} fusion(s32[8]{0:T(128)} %param.21), kind=kLoop, calls=%fused_computation.61 | loop fusion | flops 256 | bytes 288 | tf_op jit(solution)/shard_map/lt | solution.py:52
  0.8 1.0 %fusion.14 = f32[8,2,1,16]{3,2,1,0:T(1,128)S(1)} fusion(bf16[8,2,16,128]{3,0,2,1:T(8,128)(2,1)} %bitcast.59, bf16[8,2,128,1]{2,1,0,3:T(2,128)(2,1)} %bitcast.67), kind=kOutput, calls=%fused_computation.27 | convolution fusion | flops 65536 | bytes 70656 | tf_op jit(solution)/shard_map/rgjd,rgd->rgj/dot_general | solution.py:49
  1.8 1.2 %fusion.37 = (f32[8,2,16]{2,1,0:T(2,128)S(1)}, f32[8,2,16,32]{3,2,1,0:T(8,128)S(1)}) fusion(bf16[8,2,32,128]{3,2,1,0:T(8,128)(2,1)} %param.17, bf16[8,2,16,128]{3,0,2,1:T(8,128)(2,1)S(1)} %bitcast.60, pred[8,32]{1,0:T(8,128)(4,1)S(1)} %iota_compare_fusion), kind=kOutput, calls=%fused_computation.77 | convolution fusion | flops 2121472 | bytes 230656 | tf_op jit(solution)/shard_map/rgjd,rgpd->rgjp/dot_general | solution.py:45
  3.0 0.0 copy-start.9
  3.0 0.2 fusion.9
  3.3 0.0 copy-start.8
  3.3 0.7 %copy-done.8 = bf16[8,2,128]{2,1,0:T(2,128)(2,1)S(1)} copy-done((bf16[8,2,128]{2,1,0:T(2,128)(2,1)S(1)}, bf16[8,2,128]{2,1,0:T(2,128)(2,1)}, u32[]{:S(2)}) %copy-start.8) | copy-done | bytes 4120
  4.0 0.0 copy-start.6
  4.0 0.3 convolution_add_fusion
  4.2 0.0 copy-start.7
  4.2 0.5 %copy-done.5 = bf16[8,4096]{1,0:T(8,128)(2,1)S(1)} copy-done((bf16[8,4096]{1,0:T(8,128)(2,1)S(1)}, bf16[8,4096]{1,0:T(8,128)(2,1)}, u32[]{:S(2)}) %copy-start.5) | copy-done | bytes 65560
  4.8 0.2 fusion.3
  5.0 0.5 %collective-permute-start = (f32[8]{0:T(128)S(1)}, f32[8]{0:T(128)S(1)}, u32[]{:S(2)}, u32[]{:S(2)}) collective-permute-start(f32[8]{0:T(128)S(1)} %get-tuple-element.5), channel_id=1, source_target_pairs={{0,1},{1,0},{2,3},{3,2},{4,5},{5,4},{6,7},{7,6},{8,9},{9,8},{10,11... | collective-permute-start | bytes 104 | tf_op jit(solution)/shard_map/ppermute | solution.py:29
  5.5 0.2 reduce_window_sum.11
  5.7 0.6 %collective-permute-done = f32[8]{0:T(128)S(1)} collective-permute-done((f32[8]{0:T(128)S(1)}, f32[8]{0:T(128)S(1)}, u32[]{:S(2)}, u32[]{:S(2)}) %collective-permute-start) | collective-permute-done | bytes 64 | tf_op jit(solution)/shard_map/ppermute | solution.py:29
  6.3 0.1 fusion.5
  6.4 0.4 collective-permute-start.1
  6.8 0.9 %collective-permute-done.1 = bf16[8,4096]{1,0:T(8,128)(2,1)S(1)} collective-permute-done((bf16[8,4096]{1,0:T(8,128)(2,1)S(1)}, bf16[8,4096]{1,0:T(8,128)(2,1)S(1)}, u32[]{:S(2)}, u32[]{:S(2)}) %collective-permute-start.1) | collective-permute-done | bytes 65568 | tf_op jit(solution)/shard_map/ppermute | solution.py:29
  7.7 0.2 convolution_convert_fusion
  8.0 0.9 %all_to_all.8 = bf16[8,2,8192]{2,1,0:T(2,128)(2,1)} reshape(bf16[16,8192]{1,0:T(8,128)(2,1)S(1)} %convolution_convert_fusion) | data formatting | bytes 524288 | tf_op jit(solution)/shard_map/all_to_all | solution.py:132
  8.8 7.1 %all-to-all-start = ((bf16[8,2,8192]{2,1,0:T(2,128)(2,1)}), bf16[8,2,8192]{2,1,0:T(2,128)(2,1)S(1)}, u32[]{:S(2)}, u32[]{:S(2)}) async-start(bf16[8,2,8192]{2,1,0:T(2,128)(2,1)} %all_to_all.8), calls=%async_computation | async-start | bytes 524288 | tf_op jit(solution)/shard_map/all_to_all | solution.py:132
  16.0 0.4 fusion.34
  16.4 8.9 %all-to-all-done = bf16[8,2,8192]{2,1,0:T(2,128)(2,1)S(1)} async-done(((bf16[8,2,8192]{2,1,0:T(2,128)(2,1)}), bf16[8,2,8192]{2,1,0:T(2,128)(2,1)S(1)}, u32[]{:S(2)}, u32[]{:S(2)}) %all-to-all-start) | async-done | bytes 262176 | tf_op jit(solution)/shard_map/all_to_all | solution.py:132
  25.2 0.1 all_to_all.10
  25.4 0.2 fusion.38
  25.6 1.9 %fusion.2 = f32[16,8192]{1,0:T(8,128)S(1)} fusion(bf16[32,8192]{1,0:T(8,128)(2,1)} %param.28, bf16[16,8192]{1,0:T(8,128)(2,1)S(1)} %all_to_all.10, bf16[32,8192]{1,0:T(8,128)(2,1)} %param.27, f32[16,32]{1,0:T(8,128)S(1)} %fusion.38), kind=kOutput, calls=%fused_computation.7 | convolution fusion | flops 16780288 | bytes 1837056 | tf_op jit(solution)/shard_map/dot_general | solution.py:76
  27.5 0.1 collective-permute-start.3
  27.6 0.9 %fusion.27 = f32[8,8192]{1,0:T(8,128)S(1)} fusion(bf16[64,8192]{1,0:T(8,128)(2,1)S(1)} %copy-done, f32[8,64]{1,0:T(8,128)S(1)} %fusion.34, bf16[64,8192]{1,0:T(8,128)(2,1)S(1)} %copy-done.2, bf16[8,4096]{1,0:T(8,128)(2,1)S(1)} %collective-permute-done.1, bf16[8,4096]{1,0:T(8,128)(2,1)S(1)} %fusion.5, pred[]{:T(512)S(6)} %eq.16), kind=kOutput, calls=%fused_computation.66 | convolution fusion | flops 17370112 | bytes 2492417 | tf_op jit(solution)/shard_map/dot_general | solution.py:76
  28.5 0.7 %collective-permute-done.3 = f32[16,4096]{1,0:T(8,128)} collective-permute-done((f32[16,4096]{1,0:T(8,128)S(1)}, f32[16,4096]{1,0:T(8,128)}, u32[]{:S(2)}, u32[]{:S(2)}) %collective-permute-start.3) | collective-permute-done | bytes 262176 | tf_op jit(solution)/shard_map/ppermute | solution.py:29
  29.2 1.0 %dynamic-slice_add_fusion = f32[16,4096]{1,0:T(8,128)S(1)} fusion(f32[16,4096]{1,0:T(8,128)} %collective-permute-done.3, f32[16,8192]{1,0:T(8,128)S(1)} %fusion.2, s32[]{:T(128)S(6)} %select_n.61), kind=kLoop, calls=%fused_computation.8 | loop fusion | flops 65536 | bytes 786436 | tf_op jit(solution)/shard_map/add | solution.py:137
  30.2 0.2 reshape.59
  30.4 1.5 %collective-permute-start.4 = (f32[2,4096]{1,0:T(2,128)S(1)}, f32[2,4096]{1,0:T(2,128)S(1)}, u32[]{:S(2)}, u32[]{:S(2)}) collective-permute-start(f32[2,4096]{1,0:T(2,128)S(1)} %get-tuple-element.13), channel_id=1, source_target_pairs={{0,2},{2,0},{4,6},{6,4},{8,10},{10,8},{12,14},{14,12},{1,3},{3,1},... | collective-permute-start | bytes 98312 | tf_op jit(solution)/shard_map/ppermute | solution.py:143
  31.9 0.1 collective-permute-start.2
  32.0 0.1 collective-permute-start.5
  32.1 2.0 %collective-permute-start.6 = (f32[2,4096]{1,0:T(2,128)S(1)}, f32[2,4096]{1,0:T(2,128)S(1)}, u32[]{:S(2)}, u32[]{:S(2)}) collective-permute-start(f32[2,4096]{1,0:T(2,128)S(1)} %get-tuple-element.11), channel_id=1, source_target_pairs={{0,6},{2,4},{4,2},{6,0},{8,14},{10,12},{12,10},{14,8},{1,7},{3,5},... | collective-permute-start | bytes 98312 | tf_op jit(solution)/shard_map/ppermute | solution.py:143
  34.1 1.0 %collective-permute-start.7 = (f32[2,4096]{1,0:T(2,128)S(1)}, f32[2,4096]{1,0:T(2,128)S(1)}, u32[]{:S(2)}, u32[]{:S(2)}) collective-permute-start(f32[2,4096]{1,0:T(2,128)S(1)} %get-tuple-element.10), channel_id=1, source_target_pairs={{0,8},{2,10},{4,12},{6,14},{8,0},{10,2},{12,4},{14,6},{1,9},{3,11}... | collective-permute-start | bytes 98312 | tf_op jit(solution)/shard_map/ppermute | solution.py:143
  35.2 0.0 collective-permute-done.4
  35.2 2.7 %collective-permute-start.8 = (f32[2,4096]{1,0:T(2,128)S(1)}, f32[2,4096]{1,0:T(2,128)S(1)}, u32[]{:S(2)}, u32[]{:S(2)}) collective-permute-start(f32[2,4096]{1,0:T(2,128)S(1)} %get-tuple-element.9), channel_id=1, source_target_pairs={{0,10},{2,8},{4,14},{6,12},{8,2},{10,0},{12,6},{14,4},{1,11},{3,9}... | collective-permute-start | bytes 98312 | tf_op jit(solution)/shard_map/ppermute | solution.py:143
  37.9 0.0 collective-permute-done.5
  37.9 1.5 %collective-permute-start.9 = (f32[2,4096]{1,0:T(2,128)S(1)}, f32[2,4096]{1,0:T(2,128)S(1)}, u32[]{:S(2)}, u32[]{:S(2)}) collective-permute-start(f32[2,4096]{1,0:T(2,128)S(1)} %get-tuple-element.8), channel_id=1, source_target_pairs={{0,12},{2,14},{4,8},{6,10},{8,4},{10,6},{12,0},{14,2},{1,13},{3,15... | collective-permute-start | bytes 98312 | tf_op jit(solution)/shard_map/ppermute | solution.py:143
  39.5 0.0 collective-permute-done.6
  39.5 2.5 %collective-permute-start.10 = (f32[2,4096]{1,0:T(2,128)S(1)}, f32[2,4096]{1,0:T(2,128)S(1)}, u32[]{:S(2)}, u32[]{:S(2)}) collective-permute-start(f32[2,4096]{1,0:T(2,128)S(1)} %get-tuple-element.7), channel_id=1, source_target_pairs={{0,14},{2,12},{4,10},{6,8},{8,6},{10,4},{12,2},{14,0},{1,15},{3,13... | collective-permute-start | bytes 98312 | tf_op jit(solution)/shard_map/ppermute | solution.py:143
  42.0 0.0 collective-permute-done.7
  42.0 1.7 %collective-permute-done.9 = f32[2,4096]{1,0:T(2,128)S(1)} collective-permute-done((f32[2,4096]{1,0:T(2,128)S(1)}, f32[2,4096]{1,0:T(2,128)S(1)}, u32[]{:S(2)}, u32[]{:S(2)}) %collective-permute-start.9) | collective-permute-done | bytes 32800 | tf_op jit(solution)/shard_map/ppermute | solution.py:143
  43.7 2.4 %collective-permute-done.10 = f32[2,4096]{1,0:T(2,128)S(1)} collective-permute-done((f32[2,4096]{1,0:T(2,128)S(1)}, f32[2,4096]{1,0:T(2,128)S(1)}, u32[]{:S(2)}, u32[]{:S(2)}) %collective-permute-start.10) | collective-permute-done | bytes 32800 | tf_op jit(solution)/shard_map/ppermute | solution.py:143
  46.2 0.8 %gather_fusion = f32[8,2,4096]{2,1,0:T(2,128)S(1)} fusion(f32[8,2,4096]{2,1,0:T(2,128)S(1)} %bitcast_dynamic-update-slice_fusion, s32[1024]{0:T(1024)S(1)} %pad_clamp_fusion), kind=kCustom, calls=%fused_computation | custom fusion | bytes 524320 | tf_op jit(solution)/shard_map/gather | solution.py:144
  47.0 0.2 reshape.60
  47.2 1.0 %fusion.7 = bf16[8,4096]{1,0:T(8,128)(2,1)} fusion(bf16[8,4096]{1,0:T(8,128)(2,1)S(1)} %get-tuple-element.6, f32[8,4096]{1,0:T(8,128)S(1)} %collective-permute-done.2, f32[8,8192]{1,0:T(8,128)S(1)} %fusion.27, s32[]{:T(128)S(6)} %select_n.61, f32[16,8]{1,0:T(8,128)S(1)} %bitcast.61, f32[16,4096]{1,0:T(8,128)S(1)} %reshape.60), kind=kOutput, calls=%fused_computation.16 | convolution fusion | flops 6455296 | bytes 655876 | tf_op jit(solution)/shard_map/dot_general | solution.py:80
  (37 shorter events, 0.3 us)
Async XLA Ops:
  0.0 27.6 %copy-start = (bf16[64,8192]{1,0:T(8,128)(2,1)S(1)}, bf16[64,8192]{1,0:T(8,128)(2,1)}, u32[]{:S(2)}) copy-start(bf16[64,8192]{1,0:T(8,128)(2,1)} %param.25) | copy-start | bytes 3145732
  0.0 1.8 %copy-start.4 = (bf16[8,4096]{1,0:T(8,128)(2,1)S(1)}, bf16[8,4096]{1,0:T(8,128)(2,1)}, u32[]{:S(2)}) copy-start(bf16[8,4096]{1,0:T(8,128)(2,1)} %param.16) | copy-start | bytes 196612
  3.0 1.0 %copy-start.9 = (bf16[8,2,32,128]{3,2,1,0:T(8,128)(2,1)S(1)}, bf16[8,2,32,128]{3,2,1,0:T(8,128)(2,1)}, u32[]{:S(2)}) copy-start(bf16[8,2,32,128]{3,2,1,0:T(8,128)(2,1)} %param.18) | copy-start | bytes 393220
  3.3 0.7 %copy-start.8 = (bf16[8,2,128]{2,1,0:T(2,128)(2,1)S(1)}, bf16[8,2,128]{2,1,0:T(2,128)(2,1)}, u32[]{:S(2)}) copy-start(bf16[8,2,128]{2,1,0:T(2,128)(2,1)} %param.20) | copy-start | bytes 12292
  4.0 0.8 %copy-start.5 = (bf16[8,4096]{1,0:T(8,128)(2,1)S(1)}, bf16[8,4096]{1,0:T(8,128)(2,1)}, u32[]{:S(2)}) copy-start(bf16[8,4096]{1,0:T(8,128)(2,1)} %param.15) | copy-start | bytes 196612
  4.0 1.5 %copy-start.6 = (s32[8,4]{0,1:T(4,128)S(1)}, s32[8,4]{0,1:T(4,128)}, u32[]{:S(2)}) copy-start(s32[8,4]{0,1:T(4,128)} %param.29) | copy-start | bytes 388
  4.2 1.5 %copy-start.7 = (bf16[8192]{0:T(1024)(128)(2,1)S(1)}, bf16[8192]{0:T(1024)(128)(2,1)}, u32[]{:S(2)}) copy-start(bf16[8192]{0:T(1024)(128)(2,1)} %param.22) | copy-start | bytes 49156
  4.8 11.2 %copy-start.1 = (bf16[64,8192]{1,0:T(8,128)(2,1)S(1)}, bf16[64,8192]{1,0:T(8,128)(2,1)}, u32[]{:S(2)}) copy-start(bf16[64,8192]{1,0:T(8,128)(2,1)} %param.24) | copy-start | bytes 3145732
  5.0 1.3 %collective-permute-start = (f32[8]{0:T(128)S(1)}, f32[8]{0:T(128)S(1)}, u32[]{:S(2)}, u32[]{:S(2)}) collective-permute-start(f32[8]{0:T(128)S(1)} %get-tuple-element.5), channel_id=1, source_target_pairs={{0,1},{1,0},{2,3},{3,2},{4,5},{5,4},{6,7},{7,6},{8,9},{9,8},{10,11... | collective-permute-start | bytes 104 | tf_op jit(solution)/shard_map/ppermute | solution.py:29
  6.4 1.3 %collective-permute-start.1 = (bf16[8,4096]{1,0:T(8,128)(2,1)S(1)}, bf16[8,4096]{1,0:T(8,128)(2,1)S(1)}, u32[]{:S(2)}, u32[]{:S(2)}) collective-permute-start(bf16[8,4096]{1,0:T(8,128)(2,1)S(1)} %fusion.5), channel_id=1, source_target_pairs={{0,1},{1,0},{2,3},{3,2},{4,5},{5,4},{6,7},{7,6},{8,9},{9,8},{10,11... | collective-permute-start | bytes 196616 | tf_op jit(solution)/shard_map/ppermute | solution.py:29
  8.8 16.4 %all-to-all-start = ((bf16[8,2,8192]{2,1,0:T(2,128)(2,1)}), bf16[8,2,8192]{2,1,0:T(2,128)(2,1)S(1)}, u32[]{:S(2)}, u32[]{:S(2)}) async-start(bf16[8,2,8192]{2,1,0:T(2,128)(2,1)} %all_to_all.8), calls=%async_computation | async-start | bytes 524288 | tf_op jit(solution)/shard_map/all_to_all | solution.py:132
  16.4 9.0 %copy-start.3 = (bf16[32,8192]{1,0:T(8,128)(2,1)S(1)}, bf16[32,8192]{1,0:T(8,128)(2,1)}, u32[]{:S(2)}) copy-start(bf16[32,8192]{1,0:T(8,128)(2,1)} %param.26) | copy-start | bytes 1572868
  25.6 2.0 %copy-start.2 = (bf16[64,8192]{1,0:T(8,128)(2,1)S(1)}, bf16[64,8192]{1,0:T(8,128)(2,1)}, u32[]{:S(2)}) copy-start(bf16[64,8192]{1,0:T(8,128)(2,1)} %param.23) | copy-start | bytes 3145732
  27.5 1.7 %collective-permute-start.3 = (f32[16,4096]{1,0:T(8,128)S(1)}, f32[16,4096]{1,0:T(8,128)}, u32[]{:S(2)}, u32[]{:S(2)}) collective-permute-start(f32[16,4096]{1,0:T(8,128)S(1)} %constant_dynamic-slice_fusion), channel_id=1, source_target_pairs={{0,1},{1,0},{2,3},{3,2},{4,5},{5,4},{6,7},{7,6},{8,9},{9,8},{10,11... | collective-permute-start | bytes 786440 | tf_op jit(solution)/shard_map/ppermute | solution.py:29
  30.4 4.8 %collective-permute-start.4 = (f32[2,4096]{1,0:T(2,128)S(1)}, f32[2,4096]{1,0:T(2,128)S(1)}, u32[]{:S(2)}, u32[]{:S(2)}) collective-permute-start(f32[2,4096]{1,0:T(2,128)S(1)} %get-tuple-element.13), channel_id=1, source_target_pairs={{0,2},{2,0},{4,6},{6,4},{8,10},{10,8},{12,14},{14,12},{1,3},{3,1},... | collective-permute-start | bytes 98312 | tf_op jit(solution)/shard_map/ppermute | solution.py:143
  31.9 15.3 %collective-permute-start.2 = (f32[8,4096]{1,0:T(8,128)S(1)}, f32[8,4096]{1,0:T(8,128)S(1)}, u32[]{:S(2)}, u32[]{:S(2)}) collective-permute-start(f32[8,4096]{1,0:T(8,128)S(1)} %constant_dynamic-slice_fusion.1), channel_id=1, source_target_pairs={{0,1},{1,0},{2,3},{3,2},{4,5},{5,4},{6,7},{7,6},{8,9},{9,8},{10,11... | collective-permute-start | bytes 393224 | tf_op jit(solution)/shard_map/ppermute | solution.py:29
  32.0 5.9 %collective-permute-start.5 = (f32[2,4096]{1,0:T(2,128)S(1)}, f32[2,4096]{1,0:T(2,128)S(1)}, u32[]{:S(2)}, u32[]{:S(2)}) collective-permute-start(f32[2,4096]{1,0:T(2,128)S(1)} %get-tuple-element.12), channel_id=1, source_target_pairs={{0,4},{2,6},{4,0},{6,2},{8,12},{10,14},{12,8},{14,10},{1,5},{3,7},... | collective-permute-start | bytes 98312 | tf_op jit(solution)/shard_map/ppermute | solution.py:143
  32.1 7.3 %collective-permute-start.6 = (f32[2,4096]{1,0:T(2,128)S(1)}, f32[2,4096]{1,0:T(2,128)S(1)}, u32[]{:S(2)}, u32[]{:S(2)}) collective-permute-start(f32[2,4096]{1,0:T(2,128)S(1)} %get-tuple-element.11), channel_id=1, source_target_pairs={{0,6},{2,4},{4,2},{6,0},{8,14},{10,12},{12,10},{14,8},{1,7},{3,5},... | collective-permute-start | bytes 98312 | tf_op jit(solution)/shard_map/ppermute | solution.py:143
  34.1 7.8 %collective-permute-start.7 = (f32[2,4096]{1,0:T(2,128)S(1)}, f32[2,4096]{1,0:T(2,128)S(1)}, u32[]{:S(2)}, u32[]{:S(2)}) collective-permute-start(f32[2,4096]{1,0:T(2,128)S(1)} %get-tuple-element.10), channel_id=1, source_target_pairs={{0,8},{2,10},{4,12},{6,14},{8,0},{10,2},{12,4},{14,6},{1,9},{3,11}... | collective-permute-start | bytes 98312 | tf_op jit(solution)/shard_map/ppermute | solution.py:143
  35.2 6.8 %collective-permute-start.8 = (f32[2,4096]{1,0:T(2,128)S(1)}, f32[2,4096]{1,0:T(2,128)S(1)}, u32[]{:S(2)}, u32[]{:S(2)}) collective-permute-start(f32[2,4096]{1,0:T(2,128)S(1)} %get-tuple-element.9), channel_id=1, source_target_pairs={{0,10},{2,8},{4,14},{6,12},{8,2},{10,0},{12,6},{14,4},{1,11},{3,9}... | collective-permute-start | bytes 98312 | tf_op jit(solution)/shard_map/ppermute | solution.py:143
  37.9 5.8 %collective-permute-start.9 = (f32[2,4096]{1,0:T(2,128)S(1)}, f32[2,4096]{1,0:T(2,128)S(1)}, u32[]{:S(2)}, u32[]{:S(2)}) collective-permute-start(f32[2,4096]{1,0:T(2,128)S(1)} %get-tuple-element.8), channel_id=1, source_target_pairs={{0,12},{2,14},{4,8},{6,10},{8,4},{10,6},{12,0},{14,2},{1,13},{3,15... | collective-permute-start | bytes 98312 | tf_op jit(solution)/shard_map/ppermute | solution.py:143
  39.5 6.7 %collective-permute-start.10 = (f32[2,4096]{1,0:T(2,128)S(1)}, f32[2,4096]{1,0:T(2,128)S(1)}, u32[]{:S(2)}, u32[]{:S(2)}) collective-permute-start(f32[2,4096]{1,0:T(2,128)S(1)} %get-tuple-element.7), channel_id=1, source_target_pairs={{0,14},{2,12},{4,10},{6,8},{8,6},{10,4},{12,2},{14,0},{1,15},{3,13... | collective-permute-start | bytes 98312 | tf_op jit(solution)/shard_map/ppermute | solution.py:143
